TPU v7x, 32 devices: a whole 2x2x4 slice. The times are simulated.
32 devices in a mesh: lon: 4 (over x, core), lat: 8 (over z, y).
Axes of the slice: x: 2, y: 2, z: 4, core: 2. Of those that a mesh axis runs over, the one named last changes fastest.
Arguments:
- prognostic: float32 [4, 16, 192, 1536], P(None, None, 'lat', 'lon'), may hold values from -6 to 6
- tracers: float32 [4, 16, 192, 1536], P(None, None, 'lat', 'lon'), may hold values from -6 to 6
- zonal_courant: float32 [16, 192, 1536], P(None, 'lat', 'lon'), may hold values from -0.45 to 0.45
- meridional_courant: float32 [16, 192, 1536], P(None, 'lat', 'lon'), may hold values from -0.45 to 0.45
- filter_band: int32 [192], P('lat'), may hold values from 96 to 768, as said below
- dep_owner: int32 [192, 2], P('lat'), may hold values from 0 to 7, as said below
- dep_row: int32 [192, 2], P('lat'), may hold values from 0 to 23
- dep_weight: float32 [192, 2], P('lat'), may hold values from 0 to 1, as said below
Outputs:
- new_prognostic: float32 [4, 16, 192, 1536], P(None, None, 'lat', 'lon')
- new_tracers: float32 [4, 16, 192, 1536], P(None, None, 'lat', 'lon')
Inputs may be any that keep to these rules, and one draw needn't show every extreme that they name: `filter_band`: rows within 24 of either pole hold values below 768; all other rows hold 768. `dep_owner`: among the 48 entries of one band, at most 12 name the same owner band, and some owner is named exactly 12 times; the owners a band names are the bands nearest to it, distance counted across either pole. `dep_weight`: Positive; the 2 weights of a row sum to 1.
All inputs are finite; a program needn't handle non-finite values.
Results may differ from a plain program's by a relative error of at most 0.00007.
Values sent between devices are 32-bit elements; how exact they have to be, the bound alone decides.
No kernel may reach another device: no remote copies, remote signals or barrier semaphores. Data moves between devices by JAX's collectives and lax.ppermute only.
A program may use at most 128 MiB of HBM per device.

v0:
```python
import math
import jax
import jax.numpy as jnp
from jax import lax
from jax.sharding import PartitionSpec as P

PRECISE = lax.Precision.HIGHEST


def padded(value, sides, width, wrap):
    for axis, dim in sides:
        size, length = (lax.axis_size(axis), value.shape[dim])
        up = [(i, (i + 1) % size) for i in range(size if wrap else size - 1)]
        down = [(j, i) for i, j in up]
        last = lax.slice_in_dim(value, length - width, length, axis=dim)
        first = lax.slice_in_dim(value, 0, width, axis=dim)
        before = lax.ppermute(last, axis, up)
        after = lax.ppermute(first, axis, down)
        value = jnp.concatenate([before, value, after], axis=dim)
    return value


def face_flux(values, speeds, axis):
    count = values.shape[axis] - 2
    left_cells = lax.slice_in_dim(values, 0, count + 1, axis=axis)
    right_cells = lax.slice_in_dim(values, 1, count + 2, axis=axis)
    courant = lax.slice_in_dim(speeds, 0, count + 1, axis=axis)
    return 0.5 * courant * (left_cells + right_cells) - 0.5 * courant * courant * (
        right_cells - left_cells
    )


def column_factors(band_rows, length):
    column = jnp.arange(length, dtype=jnp.int32)
    half_length = length // 2
    frequency = jnp.where(column <= half_length, column, column - half_length)
    single = (column == 0) | (column == half_length)
    weights = jnp.where(single, 1.0 / length, 2.0 / length).astype(jnp.float32)
    ratios = (
        band_rows.astype(jnp.float32)[:, None]
        / jnp.maximum(frequency, 1).astype(jnp.float32)[None, :]
    )
    damping = jnp.minimum(1.0, ratios * ratios)
    return (damping - 1.0) * weights[None, :]


def circle_basis(length):
    half_length = length // 2
    column = jnp.arange(length, dtype=jnp.int32)
    frequency = jnp.where(column <= half_length, column, column - half_length)
    low_count = 64
    high_count = length // low_count
    low = jnp.arange(low_count, dtype=jnp.int32)
    high = jnp.arange(high_count, dtype=jnp.int32) * low_count
    scale = 2.0 * math.pi / length
    low_angle = scale * (low[:, None] * frequency[None, :] % length).astype(jnp.float32)
    high_angle = scale * (high[:, None] * frequency[None, :] % length).astype(jnp.float32)
    low_cos, low_sin = (jnp.cos(low_angle), jnp.sin(low_angle))
    high_cos, high_sin = (jnp.cos(high_angle), jnp.sin(high_angle))
    cos_part = high_cos[:, None] * low_cos[None] - high_sin[:, None] * low_sin[None]
    sin_part = high_sin[:, None] * low_cos[None] + high_cos[:, None] * low_sin[None]
    basis = jnp.where((column <= half_length)[None, None, :], cos_part, sin_part)
    return basis.reshape(length, length)


def polar_filter(values, band_rows):
    fields, levels, rows, block_cells = values.shape
    parts = lax.axis_size("lon")
    length = block_cells * parts
    flat = values.reshape(fields * levels * rows, block_cells)
    circles = lax.all_to_all(flat, "lon", split_axis=0, concat_axis=1, tiled=True)
    basis_table = circle_basis(length)
    spectrum = jnp.dot(circles, basis_table, precision=PRECISE)
    factors = column_factors(band_rows, length)
    circle_rows = circles.shape[0]
    scaled = (spectrum.reshape(circle_rows // rows, rows, length) * factors[None]).reshape(
        circle_rows, length
    )
    change = lax.dot_general(scaled, basis_table, (((1,), (1,)), ((), ())), precision=PRECISE)
    back = lax.all_to_all(change, "lon", split_axis=1, concat_axis=0, tiled=True)
    return values + back.reshape(values.shape)


def departure_terms(tracers, dep_owner, dep_row, dep_weight):
    band_count = lax.axis_size("lat")
    row_count, link_count = dep_owner.shape
    entries = row_count * link_count
    capacity = max(2, -(-2 * entries // band_count))
    owner_ids = dep_owner.reshape(entries)
    source = dep_row.reshape(entries)
    positions = jnp.arange(entries)
    earlier = (owner_ids[:, None] == owner_ids[None, :]) & (positions[None, :] < positions[:, None])
    slot_ids = jnp.sum(earlier.astype(jnp.int32), axis=1)
    band_ids = jnp.arange(band_count, dtype=jnp.int32)
    slot_range = jnp.arange(capacity, dtype=jnp.int32)
    matches = (owner_ids[:, None, None] == band_ids[None, :, None]) & (
        slot_ids[:, None, None] == slot_range[None, None, :]
    )
    request = jnp.sum(jnp.where(matches, source[:, None, None], 0), axis=0)
    wanted = lax.all_to_all(request, "lat", split_axis=0, concat_axis=0, tiled=True)
    by_row = jnp.transpose(tracers, (2, 0, 1, 3))
    outgoing = by_row[wanted]
    incoming = lax.all_to_all(outgoing, "lat", split_axis=0, concat_axis=0, tiled=True)
    stacked_rows = incoming.reshape((band_count * capacity,) + incoming.shape[2:])
    picked = stacked_rows[owner_ids * capacity + slot_ids].reshape(
        (row_count, link_count) + stacked_rows.shape[1:]
    )
    summed = dep_weight[:, 0][:, None, None, None] * picked[:, 0]
    summed = summed + dep_weight[:, 1][:, None, None, None] * picked[:, 1]
    return jnp.transpose(summed, (1, 2, 0, 3))


def body(
    prognostic,
    tracers,
    zonal_courant,
    meridional_courant,
    filter_band,
    dep_owner,
    dep_row,
    dep_weight,
):
    row_count = prognostic.shape[2]
    departed = departure_terms(tracers, dep_owner, dep_row, dep_weight)
    lon_padded = padded(
        jnp.concatenate([prognostic, zonal_courant[None]], axis=0), (("lon", 3),), 1, True
    )
    zonal_flux = face_flux(lon_padded[:-1], lon_padded[-1:], 3)
    lat_padded = padded(
        jnp.concatenate([prognostic, meridional_courant[None]], axis=0), (("lat", 2),), 1, False
    )
    merid_flux = face_flux(lat_padded[:-1], lat_padded[-1:], 2)
    total_rows = row_count * lax.axis_size("lat")
    face_rows = lax.axis_index("lat") * row_count + jnp.arange(row_count + 1) - 1
    merid_flux = jnp.where(
        (face_rows == total_rows - 1)[None, None, :, None], jnp.float32(0.0), merid_flux
    )
    advected = (
        prognostic
        - (zonal_flux[..., 1:] - zonal_flux[..., :-1])
        - (merid_flux[:, :, 1:] - merid_flux[:, :, :-1])
    )
    new_prognostic = polar_filter(advected, filter_band)
    return (new_prognostic, departed)


def solution(mesh):
    return jax.shard_map(
        body,
        mesh=mesh,
        in_specs=(
            P(None, None, "lat", "lon"),
            P(None, None, "lat", "lon"),
            P(None, "lat", "lon"),
            P(None, "lat", "lon"),
            P("lat"),
            P("lat", None),
            P("lat", None),
            P("lat", None),
        ),
        out_specs=(P(None, None, "lat", "lon"), P(None, None, "lat", "lon")),
        check_vma=False,
    )
```

profile of v0, /device:TPU:0, one launch (start us, length us, event | category | flops | bytes accessed | tf_op | source)
XLA Modules:
  0.0 364.4 jit_solution(3108932577473310589)
XLA Ops:
  0.7 3.3 pad_maximum_fusion.8
  10.8 4.9 %collective-permute-start.2 = (f32[5,16,1,384]{3,1,2,0:T(8,128)}, f32[5,16,1,384]{3,1,2,0:T(8,128)}, u32[]{:S(2)}, u32[]{:S(2)}) collective-permute-start(f32[5,16,1,384]{3,1,2,0:T(8,128)} %copy.61), channel_id=1, source_target_pairs={{0,1},{1,2},{2,3},{3,4},{4,5},{5,6},{6,7},{8,9},{9,10},{10,11},{11... | collective-permute-start | bytes 368648 | tf_op jit(solution)/shard_map/ppermute | solution.py:17
  20.8 2.2 multiply_bitcast_fusion.1
  24.0 2.3 copy.60
  26.3 2.7 multiply_subtract_fusion
  32.6 2.3 fusion.4
  34.9 3.6 all-to-all-start
  41.5 5.8 %add_select_fusion = f32[24,64,1536]{2,1,0:T(8,128)} fusion(f32[64,1536]{1,0:T(8,128)S(1)} %get-tuple-element.21, f32[24,1536]{1,0:T(8,128)S(1)} %get-tuple-element.19, f32[64,1536]{1,0:T(8,128)S(1)} %get-tuple-element.20, f32[24,1536]{1,0:T(8,128)S(1)} %get-tuple-element.18, pred[1536]{0:T(1024)(128)(4,1)S(1)} %iota_compare_fusion.4), kind=kLoop, calls=%fused_computation.2 | loop fusion | flops 16515072 | bytes 10520064 | tf_op jit(solution)/shard_map/jit(_where)/select_n | solution.py:62
  47.3 19.7 %all-to-all-done = f32[4,384,384]{2,1,0:T(8,128)S(1)} async-done(((f32[4,384,384]{2,1,0:T(8,128)}), f32[4,384,384]{2,1,0:T(8,128)S(1)}, u32[]{:S(2)}, u32[]{:S(2)}) %all-to-all-start) | async-done | bytes 2359328 | tf_op jit(solution)/shard_map/all_to_all | solution.py:71
  67.0 6.9 %all-to-all-start.2 = ((s32[8,1,12]{2,1,0:T(1,128)}), s32[8,1,12]{2,1,0:T(1,128)S(1)}, u32[]{:S(2)}, u32[]{:S(2)}) async-start(s32[8,1,12]{2,1,0:T(1,128)} %copy.70), calls=%async_computation.2 | async-start | bytes 8192 | tf_op jit(solution)/shard_map/all_to_all | solution.py:100
  73.9 2.9 copy.65
  76.9 2.7 dot_general.8
  79.6 14.7 %convolution_multiply_fusion = f32[16,24,1536]{2,1,0:T(8,128)S(1)} fusion(f32[16,24,1536]{2,1,0:T(8,128)S(1)} %dot_general.8, f32[1536,1536,1]{1,0,2:T(8,128)} %bitcast.64, f32[24,1536]{1,0:T(8,128)S(1)} %fusion.18), kind=kOutput, calls=%fused_computation.13 | convolution fusion | flops 10872225792 | bytes 14303232 | tf_op jit(solution)/shard_map/dot_general | solution.py:73
  94.3 13.0 %fusion.31 = f32[384,4,384]{2,0,1:T(8,128)} fusion(f32[384,1536,1]{1,0,2:T(8,128)S(1)} %bitcast.71, f32[4,384,1536]{2,1,0:T(8,128)S(1)} %bitcast.65), kind=kOutput, calls=%fused_computation.87 | convolution fusion | flops 10871635968 | bytes 14155776 | tf_op jit(solution)/shard_map/dot_general | solution.py:79
  107.3 4.8 %all-to-all-start.1 = ((f32[384,4,384]{2,0,1:T(8,128)}), f32[384,4,384]{2,0,1:T(8,128)}, u32[]{:S(2)}, u32[]{:S(2)}) async-start(f32[384,4,384]{2,0,1:T(8,128)} %fusion.31), calls=%async_computation.1 | async-start | bytes 4718592 | tf_op jit(solution)/shard_map/all_to_all | solution.py:80
  112.1 2.1 copy.78
  114.3 4.8 %gather_fusion = f32[96,4,16,384]{3,2,1,0:T(8,128)} fusion(f32[24,4,16,384]{3,2,1,0:T(8,128)S(1)} %bitcast.66, s32[1024]{0:T(1024)S(1)} %pad_clamp_fusion.1), kind=kCustom, calls=%fused_computation | custom fusion | bytes 18874752 | tf_op jit(solution)/shard_map/gather | solution.py:102
  119.1 21.3 %all-to-all-done.1 = f32[384,4,384]{2,0,1:T(8,128)} async-done(((f32[384,4,384]{2,0,1:T(8,128)}), f32[384,4,384]{2,0,1:T(8,128)}, u32[]{:S(2)}, u32[]{:S(2)}) %all-to-all-start.1) | async-done | bytes 2359328 | tf_op jit(solution)/shard_map/all_to_all | solution.py:80
  140.4 6.1 %all-to-all-start.3 = ((f32[8,12,4,16,384]{4,3,2,1,0:T(8,128)}), f32[8,12,4,16,384]{4,3,2,1,0:T(8,128)}, u32[]{:S(2)}, u32[]{:S(2)}) async-start(f32[8,12,4,16,384]{4,3,2,1,0:T(8,128)} %bitcast.67), calls=%async_computation.3 | async-start | bytes 18874368 | tf_op jit(solution)/shard_map/all_to_all | solution.py:103
  146.8 3.3 add.134
  150.1 201.9 %all-to-all-done.3 = f32[8,12,4,16,384]{4,3,2,1,0:T(8,128)} async-done(((f32[8,12,4,16,384]{4,3,2,1,0:T(8,128)}), f32[8,12,4,16,384]{4,3,2,1,0:T(8,128)}, u32[]{:S(2)}, u32[]{:S(2)}) %all-to-all-start.3) | async-done | bytes 9437216 | tf_op jit(solution)/shard_map/all_to_all | solution.py:103
  352.0 6.7 %gather_fusion.1 = f32[48,4,16,384]{3,2,1,0:T(8,128)} fusion(f32[96,4,16,384]{3,2,1,0:T(8,128)} %bitcast.20, s32[1024]{0:T(1024)S(1)} %pad_clamp_fusion), kind=kCustom, calls=%fused_computation.1 | custom fusion | bytes 9437376 | tf_op jit(solution)/shard_map/gather | solution.py:105
  358.7 2.9 fusion.2
  361.6 2.8 copy.73
  (72 shorter events, 19.6 us)
Async XLA Ops:
  0.6 9.3 %copy-start = (f32[4,16,24,384]{3,2,1,0:T(8,128)S(1)}, f32[4,16,24,384]{3,2,1,0:T(8,128)}, u32[]{:S(2)}) copy-start(f32[4,16,24,384]{3,2,1,0:T(8,128)} %param.8) | copy-start | bytes 7077892
  0.6 9.3 %copy-start.3 = (f32[16,24,384]{2,1,0:T(8,128)S(1)}, f32[16,24,384]{2,1,0:T(8,128)}, u32[]{:S(2)}) copy-start(f32[16,24,384]{2,1,0:T(8,128)} %param.11) | copy-start | bytes 1769476
  4.0 13.7 %copy-start.5 = (s32[24,2]{0,1:T(2,128)S(1)}, s32[24,2]{0,1:T(2,128)}, u32[]{:S(2)}) copy-start(s32[24,2]{0,1:T(2,128)} %param.13) | copy-start | bytes 580
  4.0 14.1 %copy-start.11 = (s32[24]{0:T(128)S(1)}, s32[24]{0:T(128)}, u32[]{:S(2)}) copy-start(s32[24]{0:T(128)} %param.12) | copy-start | bytes 292
  4.0 14.1 %copy-start.7 = (s32[24,2]{0,1:T(2,128)S(1)}, s32[24,2]{0,1:T(2,128)}, u32[]{:S(2)}) copy-start(s32[24,2]{0,1:T(2,128)} %param.14) | copy-start | bytes 580
  5.7 13.8 %collective-permute-start = (f32[5,16,24,1]{2,1,3,0:T(8,128)S(1)}, f32[5,16,24,1]{2,1,3,0:T(8,128)}, u32[]{:S(2)}, u32[]{:S(2)}) collective-permute-start(f32[5,16,24,1]{2,1,3,0:T(8,128)S(1)} %copy.57), channel_id=1, source_target_pairs={{0,8},{8,16},{16,24},{24,0},{1,9},{9,17},{17,25},{25,1},{2,10},{10... | collective-permute-start | bytes 23048 | tf_op jit(solution)/shard_map/ppermute | solution.py:17
  7.9 16.1 %collective-permute-start.1 = (f32[5,16,24,1]{2,1,3,0:T(8,128)S(1)}, f32[5,16,24,1]{2,1,3,0:T(8,128)}, u32[]{:S(2)}, u32[]{:S(2)}) collective-permute-start(f32[5,16,24,1]{2,1,3,0:T(8,128)S(1)} %copy.59), channel_id=1, source_target_pairs={{8,0},{16,8},{24,16},{0,24},{9,1},{17,9},{25,17},{1,25},{10,2},{18... | collective-permute-start | bytes 23048 | tf_op jit(solution)/shard_map/ppermute | solution.py:18
  10.8 18.3 %collective-permute-start.2 = (f32[5,16,1,384]{3,1,2,0:T(8,128)}, f32[5,16,1,384]{3,1,2,0:T(8,128)}, u32[]{:S(2)}, u32[]{:S(2)}) collective-permute-start(f32[5,16,1,384]{3,1,2,0:T(8,128)} %copy.61), channel_id=1, source_target_pairs={{0,1},{1,2},{2,3},{3,4},{4,5},{5,6},{6,7},{8,9},{9,10},{10,11},{11... | collective-permute-start | bytes 368648 | tf_op jit(solution)/shard_map/ppermute | solution.py:17
  16.3 14.1 %collective-permute-start.3 = (f32[5,16,1,384]{3,1,2,0:T(8,128)}, f32[5,16,1,384]{3,1,2,0:T(8,128)}, u32[]{:S(2)}, u32[]{:S(2)}) collective-permute-start(f32[5,16,1,384]{3,1,2,0:T(8,128)} %copy.63), channel_id=1, source_target_pairs={{1,0},{2,1},{3,2},{4,3},{5,4},{6,5},{7,6},{9,8},{10,9},{11,10},{12... | collective-permute-start | bytes 368648 | tf_op jit(solution)/shard_map/ppermute | solution.py:18
  18.0 0.6 copy-start.9
  26.3 3.8 %copy-start.4 = (f32[16,24,384]{2,1,0:T(8,128)S(1)}, f32[16,24,384]{2,1,0:T(8,128)}, u32[]{:S(2)}) copy-start(f32[16,24,384]{2,1,0:T(8,128)} %param.11) | copy-start | bytes 1769476
  30.1 1.3 copy-start.8
  34.9 32.1 %all-to-all-start = ((f32[4,384,384]{2,1,0:T(8,128)}), f32[4,384,384]{2,1,0:T(8,128)S(1)}, u32[]{:S(2)}, u32[]{:S(2)}) async-start(f32[4,384,384]{2,1,0:T(8,128)} %bitcast.68), calls=%async_computation | async-start | bytes 4718592 | tf_op jit(solution)/shard_map/all_to_all | solution.py:71
  67.0 40.3 %all-to-all-start.2 = ((s32[8,1,12]{2,1,0:T(1,128)}), s32[8,1,12]{2,1,0:T(1,128)S(1)}, u32[]{:S(2)}, u32[]{:S(2)}) async-start(s32[8,1,12]{2,1,0:T(1,128)} %copy.70), calls=%async_computation.2 | async-start | bytes 8192 | tf_op jit(solution)/shard_map/all_to_all | solution.py:100
  79.6 14.8 %copy-start.1 = (f32[24,64,1536]{2,1,0:T(8,128)S(1)}, f32[24,64,1536]{2,1,0:T(8,128)}, u32[]{:S(2)}) copy-start(f32[24,64,1536]{2,1,0:T(8,128)} %add_select_fusion) | copy-start | bytes 28311556
  107.3 33.1 %all-to-all-start.1 = ((f32[384,4,384]{2,0,1:T(8,128)}), f32[384,4,384]{2,0,1:T(8,128)}, u32[]{:S(2)}, u32[]{:S(2)}) async-start(f32[384,4,384]{2,0,1:T(8,128)} %fusion.31), calls=%async_computation.1 | async-start | bytes 4718592 | tf_op jit(solution)/shard_map/all_to_all | solution.py:80
  140.4 6.3 %copy-start.10 = (s32[48]{0:T(128)S(1)}, s32[48]{0:T(128)}, u32[]{:S(2)}) copy-start(s32[48]{0:T(128)} %copy-done.9) | copy-start | bytes 580
  140.4 6.4 %copy-start.6 = (f32[24,2]{0,1:T(2,128)S(1)}, f32[24,2]{0,1:T(2,128)}, u32[]{:S(2)}) copy-start(f32[24,2]{0,1:T(2,128)} %param.15) | copy-start | bytes 580
  140.4 6.4 %copy-start.2 = (f32[4,16,24,384]{3,2,1,0:T(8,128)S(1)}, f32[4,16,24,384]{3,2,1,0:T(8,128)}, u32[]{:S(2)}) copy-start(f32[4,16,24,384]{3,2,1,0:T(8,128)} %fusion.4) | copy-start | bytes 7077892
  140.4 211.6 %all-to-all-start.3 = ((f32[8,12,4,16,384]{4,3,2,1,0:T(8,128)}), f32[8,12,4,16,384]{4,3,2,1,0:T(8,128)}, u32[]{:S(2)}, u32[]{:S(2)}) async-start(f32[8,12,4,16,384]{4,3,2,1,0:T(8,128)} %bitcast.67), calls=%async_computation.3 | async-start | bytes 18874368 | tf_op jit(solution)/shard_map/all_to_all | solution.py:103
where the time goes:
time: 365 us; the launch traced here: 364 us
  waiting for transfers between devices  243 us (67%)
  local copies, waits for them, and re-layouts  34.2 us (9%)
  starting transfers between devices  30.1 us (8%)
  other arithmetic  28.6 us (8%)
  matrix products  27.7 us (8%)
    all_to_all x1, waiting for transfers between devices, departure_terms(): lax.all_to_all(outgoing, 'lat', split_axis=0, concat_axis=0, tiled=True)  202 us
    all_to_all x1, waiting for transfers between devices, polar_filter(): lax.all_to_all(change, 'lon', split_axis=1, concat_axis=0, tiled=True)  21.3 us
    all_to_all x1, waiting for transfers between devices, polar_filter(): lax.all_to_all(flat, 'lon', split_axis=0, concat_axis=1, tiled=True)  19.7 us
    dot_general x1, matrix products, polar_filter(): spectrum = jnp.dot(circles, basis_table, precision=PRECISE)  14.7 us
    dot_general x1, matrix products, polar_filter(): lax.dot_general(scaled, basis_table, (((1,), (1,)), ((), ())), precision=...  13 us
  transfers between devices with their start and end apart: 8, of which 3 were waited for; matrix products, arithmetic and copies ran while one was open for 19% of the time, Pallas kernels for 0%

commit v1 on v0

--- a/solution.py
+++ b/solution.py
@@ -5,6 +5,18 @@
 from jax.sharding import PartitionSpec as P
 
 PRECISE = lax.Precision.HIGHEST
+
+
+def exchange_directly(array, axis, split, join):
+    ways, here = (lax.axis_size(axis), lax.axis_index(axis))
+    width = array.shape[split] // ways
+    turned = jnp.roll(array, -here * width, axis=split)
+    got = [lax.slice_in_dim(turned, 0, width, axis=split)]
+    for far in range(1, ways):
+        sent = lax.slice_in_dim(turned, far * width, (far + 1) * width, axis=split)
+        got.append(lax.ppermute(sent, axis, [(d, (d + far) % ways) for d in range(ways)]))
+    line = jnp.concatenate(got[::-1], axis=join)
+    return jnp.roll(line, (here + 1) * got[0].shape[join], axis=join)
 
 
 def padded(value, sides, width, wrap):
@@ -77,7 +89,7 @@
         circle_rows, length
     )
     change = lax.dot_general(scaled, basis_table, (((1,), (1,)), ((), ())), precision=PRECISE)
-    back = lax.all_to_all(change, "lon", split_axis=1, concat_axis=0, tiled=True)
+    back = exchange_directly(change, "lon", 1, 0)
     return values + back.reshape(values.shape)
 
 

time: 365 us -> 298 us (0.82)
  waiting for transfers between devices: 243 us -> 176 us
    all_to_all x1, waiting for transfers between devices: 202 us -> 131 us  [departure_terms(): lax.all_to_all(outgoing, 'lat', split_axis=0, concat_axis=0, tiled=True)]
    ppermute x0 -> x3, waiting for transfers between devices: none -> 24 us  [exchange_directly(): lax.ppermute(sent, axis, [(d, (d + far) % ways) for d in range(ways)])]
    all_to_all x1 -> x0, waiting for transfers between devices: 21.3 us -> none  [polar_filter(): lax.all_to_all(change, 'lon', split_axis=1, concat_axis=0, tiled=True)]
    all_to_all x1 -> x0, starting transfers between devices: 4.78 us -> none  [polar_filter(): lax.all_to_all(change, 'lon', split_axis=1, concat_axis=0, tiled=True)]
    unnamed x28 -> x31, local copies, waits for them, and re-layouts: 5.44 us -> 7.38 us
  transfers between devices with their start and end apart: 8 -> 10, of which waited for: 3 -> 5; matrix products, arithmetic and copies ran while one was open for 19% -> 25% of each run, Pallas kernels for 0% -> 0%
where the time goes in v1:
time: 298 us; the launch traced here: 297 us
  waiting for transfers between devices  176 us (59%)
  local copies, waits for them, and re-layouts  36.4 us (12%)
  other arithmetic  29.2 us (10%)
  starting transfers between devices  27.2 us (9%)
  matrix products  27.1 us (9%)
    all_to_all x1, waiting for transfers between devices, departure_terms(): lax.all_to_all(outgoing, 'lat', split_axis=0, concat_axis=0, tiled=True)  131 us
    ppermute x3, waiting for transfers between devices, exchange_directly(): lax.ppermute(sent, axis, [(d, (d + far) % ways) for d in range(ways)])  24 us
    all_to_all x1, waiting for transfers between devices, polar_filter(): lax.all_to_all(flat, 'lon', split_axis=0, concat_axis=1, tiled=True)  21.5 us
    dot_general x1, matrix products, polar_filter(): spectrum = jnp.dot(circles, basis_table, precision=PRECISE)  15.5 us
    dot_general x1, matrix products, polar_filter(): lax.dot_general(scaled, basis_table, (((1,), (1,)), ((), ())), precision=...  11.6 us
    unnamed x31, local copies, waits for them, and re-layouts  7.38 us
    all_to_all x1, starting transfers between devices, departure_terms(): lax.all_to_all(request, 'lat', split_axis=0, concat_axis=0, tiled=True)  6.93 us
    gather x1, local copies, waits for them, and re-layouts, departure_terms(): stacked_rows[owner_ids * capacity + slot_ids]  6.74 us
  transfers between devices with their start and end apart: 10, of which 5 were waited for; matrix products, arithmetic and copies ran while one was open for 25% of the time, Pallas kernels for 0%

profile of v1, /device:TPU:0, one launch (start us, length us, event | category | flops | bytes accessed | tf_op | source)
XLA Modules:
  0.0 297.3 jit_solution(7615266740120763442)
XLA Ops:
  0.7 1.9 pad_maximum_fusion.11
  3.2 5.5 %collective-permute-start.2 = (f32[5,16,1,384]{3,1,2,0:T(8,128)}, f32[5,16,1,384]{3,1,2,0:T(8,128)}, u32[]{:S(2)}, u32[]{:S(2)}) collective-permute-start(f32[5,16,1,384]{3,1,2,0:T(8,128)} %copy.60), channel_id=1, source_target_pairs={{0,1},{1,2},{2,3},{3,4},{4,5},{5,6},{6,7},{8,9},{9,10},{10,11},{11... | collective-permute-start | bytes 368648 | tf_op jit(solution)/shard_map/ppermute | solution.py:29
  11.4 2.4 copy.56
  18.2 6.9 %all-to-all-start.1 = ((s32[8,1,12]{2,1,0:T(1,128)}), s32[8,1,12]{2,1,0:T(1,128)S(1)}, u32[]{:S(2)}, u32[]{:S(2)}) async-start(s32[8,1,12]{2,1,0:T(1,128)} %copy.69), calls=%async_computation.1 | async-start | bytes 8192 | tf_op jit(solution)/shard_map/all_to_all | solution.py:112
  27.0 2.2 multiply_bitcast_fusion.1
  31.7 2.7 multiply_subtract_fusion
  38.0 2.3 fusion.5
  40.3 4.5 %all-to-all-start = ((f32[4,384,384]{2,1,0:T(8,128)}), f32[4,384,384]{2,1,0:T(8,128)}, u32[]{:S(2)}, u32[]{:S(2)}) async-start(f32[4,384,384]{2,1,0:T(8,128)} %bitcast.63), calls=%async_computation | async-start | bytes 4718592 | tf_op jit(solution)/shard_map/all_to_all | solution.py:83
  44.8 2.1 copy.77
  47.0 4.8 %gather_fusion = f32[96,4,16,384]{3,2,1,0:T(8,128)} fusion(f32[24,4,16,384]{3,2,1,0:T(8,128)S(1)} %bitcast.61, s32[1024]{0:T(1024)S(1)} %pad_clamp_fusion.1), kind=kCustom, calls=%fused_computation | custom fusion | bytes 18874752 | tf_op jit(solution)/shard_map/gather | solution.py:114
  51.8 21.5 %all-to-all-done = f32[4,384,384]{2,1,0:T(8,128)} async-done(((f32[4,384,384]{2,1,0:T(8,128)}), f32[4,384,384]{2,1,0:T(8,128)}, u32[]{:S(2)}, u32[]{:S(2)}) %all-to-all-start) | async-done | bytes 2359328 | tf_op jit(solution)/shard_map/all_to_all | solution.py:83
  73.3 6.1 %all-to-all-start.2 = ((f32[8,12,4,16,384]{4,3,2,1,0:T(8,128)}), f32[8,12,4,16,384]{4,3,2,1,0:T(8,128)}, u32[]{:S(2)}, u32[]{:S(2)}) async-start(f32[8,12,4,16,384]{4,3,2,1,0:T(8,128)} %bitcast.62), calls=%async_computation.2 | async-start | bytes 18874368 | tf_op jit(solution)/shard_map/all_to_all | solution.py:115
  81.9 5.8 %add_select_fusion = f32[24,64,1536]{2,1,0:T(8,128)} fusion(f32[64,1536]{1,0:T(8,128)S(1)} %get-tuple-element.24, f32[24,1536]{1,0:T(8,128)S(1)} %get-tuple-element.22, f32[64,1536]{1,0:T(8,128)S(1)} %get-tuple-element.23, f32[24,1536]{1,0:T(8,128)S(1)} %get-tuple-element.21, pred[1536]{0:T(1024)(128)(4,1)S(1)} %iota_compare_fusion.4), kind=kLoop, calls=%fused_computation.2 | loop fusion | flops 16515072 | bytes 10520064 | tf_op jit(solution)/shard_map/jit(_where)/select_n | solution.py:74
  87.8 3.2 %copy.64 = f32[384,4,384]{2,1,0:T(4,128)S(1)} copy(f32[384,4,384]{2,0,1:T(8,128)} %bitcast.7) | data formatting | bytes 4718592 | tf_op jit(solution)/shard_map/all_to_all | solution.py:83
  90.9 2.0 dot_general.8
  92.9 15.5 %convolution_multiply_fusion = f32[16,24,1536]{2,1,0:T(8,128)S(1)} fusion(f32[16,24,1536]{2,1,0:T(8,128)} %dot_general.8, f32[1536,1536,1]{1,0,2:T(8,128)} %bitcast.59, f32[24,1536]{1,0:T(8,128)S(1)} %fusion.19), kind=kOutput, calls=%fused_computation.15 | convolution fusion | flops 10872225792 | bytes 14303232 | tf_op jit(solution)/shard_map/dot_general | solution.py:85
  108.4 11.6 %fusion.33 = f32[384,1536]{1,0:T(8,128)S(1)} fusion(f32[384,1536]{1,0:T(8,128)S(1)} %bitcast.66, f32[1536,1536]{1,0:T(8,128)S(1)} %bitcast.60), kind=kOutput, calls=%fused_computation.100 | convolution fusion | flops 10871635968 | bytes 14155776 | tf_op jit(solution)/shard_map/dot_general | solution.py:91
  126.4 8.7 %collective-permute-done.4 = f32[384,384]{1,0:T(8,128)S(1)} collective-permute-done((f32[384,384]{1,0:T(8,128)}, f32[384,384]{1,0:T(8,128)S(1)}, u32[]{:S(2)}, u32[]{:S(2)}) %collective-permute-start.4) | collective-permute-done | bytes 589856 | tf_op jit(solution)/shard_map/ppermute | solution.py:17
  135.1 13.2 %collective-permute-done.5 = f32[384,384]{1,0:T(8,128)S(1)} collective-permute-done((f32[384,384]{1,0:T(8,128)}, f32[384,384]{1,0:T(8,128)S(1)}, u32[]{:S(2)}, u32[]{:S(2)}) %collective-permute-start.5) | collective-permute-done | bytes 589856 | tf_op jit(solution)/shard_map/ppermute | solution.py:17
  148.4 2.1 collective-permute-done.6
  154.1 130.8 %all-to-all-done.2 = f32[8,12,4,16,384]{4,3,2,1,0:T(8,128)} async-done(((f32[8,12,4,16,384]{4,3,2,1,0:T(8,128)}), f32[8,12,4,16,384]{4,3,2,1,0:T(8,128)}, u32[]{:S(2)}, u32[]{:S(2)}) %all-to-all-start.2) | async-done | bytes 9437216 | tf_op jit(solution)/shard_map/all_to_all | solution.py:115
  284.9 6.7 %gather_fusion.1 = f32[48,4,16,384]{3,2,1,0:T(8,128)} fusion(f32[96,4,16,384]{3,2,1,0:T(8,128)} %bitcast.17, s32[1024]{0:T(1024)S(1)} %pad_clamp_fusion), kind=kCustom, calls=%fused_computation.1 | custom fusion | bytes 9437376 | tf_op jit(solution)/shard_map/gather | solution.py:117
  291.6 2.9 fusion.3
  294.5 2.8 copy.72
  (83 shorter events, 27.9 us)
Async XLA Ops:
  0.6 9.4 %copy-start = (f32[4,16,24,384]{3,2,1,0:T(8,128)S(1)}, f32[4,16,24,384]{3,2,1,0:T(8,128)}, u32[]{:S(2)}) copy-start(f32[4,16,24,384]{3,2,1,0:T(8,128)} %param.8) | copy-start | bytes 7077892
  0.6 9.4 %copy-start.3 = (f32[16,24,384]{2,1,0:T(8,128)S(1)}, f32[16,24,384]{2,1,0:T(8,128)}, u32[]{:S(2)}) copy-start(f32[16,24,384]{2,1,0:T(8,128)} %param.10) | copy-start | bytes 1769476
  3.2 31.2 %collective-permute-start.2 = (f32[5,16,1,384]{3,1,2,0:T(8,128)}, f32[5,16,1,384]{3,1,2,0:T(8,128)}, u32[]{:S(2)}, u32[]{:S(2)}) collective-permute-start(f32[5,16,1,384]{3,1,2,0:T(8,128)} %copy.60), channel_id=1, source_target_pairs={{0,1},{1,2},{2,3},{3,4},{4,5},{5,6},{6,7},{8,9},{9,10},{10,11},{11... | collective-permute-start | bytes 368648 | tf_op jit(solution)/shard_map/ppermute | solution.py:29
  8.7 27.0 %collective-permute-start.3 = (f32[5,16,1,384]{3,1,2,0:T(8,128)S(1)}, f32[5,16,1,384]{3,1,2,0:T(8,128)}, u32[]{:S(2)}, u32[]{:S(2)}) collective-permute-start(f32[5,16,1,384]{3,1,2,0:T(8,128)S(1)} %copy.62), channel_id=1, source_target_pairs={{1,0},{2,1},{3,2},{4,3},{5,4},{6,5},{7,6},{9,8},{10,9},{11,10},{12... | collective-permute-start | bytes 368648 | tf_op jit(solution)/shard_map/ppermute | solution.py:30
  10.1 6.0 %copy-start.5 = (s32[24,2]{0,1:T(2,128)S(1)}, s32[24,2]{0,1:T(2,128)}, u32[]{:S(2)}) copy-start(s32[24,2]{0,1:T(2,128)} %param.13) | copy-start | bytes 580
  10.1 6.9 %copy-start.6 = (s32[24,2]{0,1:T(2,128)S(1)}, s32[24,2]{0,1:T(2,128)}, u32[]{:S(2)}) copy-start(s32[24,2]{0,1:T(2,128)} %param.14) | copy-start | bytes 580
  13.7 11.9 %collective-permute-start = (f32[5,16,24,1]{2,1,3,0:T(8,128)}, f32[5,16,24,1]{2,1,3,0:T(8,128)}, u32[]{:S(2)}, u32[]{:S(2)}) collective-permute-start(f32[5,16,24,1]{2,1,3,0:T(8,128)} %copy.56), channel_id=1, source_target_pairs={{0,8},{8,16},{16,24},{24,0},{1,9},{9,17},{17,25},{25,1},{2,10},{10... | collective-permute-start | bytes 23048 | tf_op jit(solution)/shard_map/ppermute | solution.py:29
  14.2 15.9 %collective-permute-start.1 = (f32[5,16,24,1]{2,1,3,0:T(8,128)S(1)}, f32[5,16,24,1]{2,1,3,0:T(8,128)S(1)}, u32[]{:S(2)}, u32[]{:S(2)}) collective-permute-start(f32[5,16,24,1]{2,1,3,0:T(8,128)S(1)} %copy.58), channel_id=1, source_target_pairs={{8,0},{16,8},{24,16},{0,24},{9,1},{17,9},{25,17},{1,25},{10,2},{18... | collective-permute-start | bytes 23048 | tf_op jit(solution)/shard_map/ppermute | solution.py:30
  16.4 0.6 copy-start.8
  18.2 22.1 %all-to-all-start.1 = ((s32[8,1,12]{2,1,0:T(1,128)}), s32[8,1,12]{2,1,0:T(1,128)S(1)}, u32[]{:S(2)}, u32[]{:S(2)}) async-start(s32[8,1,12]{2,1,0:T(1,128)} %copy.69), calls=%async_computation.1 | async-start | bytes 8192 | tf_op jit(solution)/shard_map/all_to_all | solution.py:112
  31.6 3.8 %copy-start.4 = (f32[16,24,384]{2,1,0:T(8,128)S(1)}, f32[16,24,384]{2,1,0:T(8,128)}, u32[]{:S(2)}) copy-start(f32[16,24,384]{2,1,0:T(8,128)} %param.11) | copy-start | bytes 1769476
  35.5 1.3 copy-start.7
  40.3 33.1 %all-to-all-start = ((f32[4,384,384]{2,1,0:T(8,128)}), f32[4,384,384]{2,1,0:T(8,128)}, u32[]{:S(2)}, u32[]{:S(2)}) async-start(f32[4,384,384]{2,1,0:T(8,128)} %bitcast.63), calls=%async_computation | async-start | bytes 4718592 | tf_op jit(solution)/shard_map/all_to_all | solution.py:83
  73.3 6.1 %copy-start.9 = (s32[24]{0:T(128)S(1)}, s32[24]{0:T(128)}, u32[]{:S(2)}) copy-start(s32[24]{0:T(128)} %param.12) | copy-start | bytes 292
  73.3 211.6 %all-to-all-start.2 = ((f32[8,12,4,16,384]{4,3,2,1,0:T(8,128)}), f32[8,12,4,16,384]{4,3,2,1,0:T(8,128)}, u32[]{:S(2)}, u32[]{:S(2)}) async-start(f32[8,12,4,16,384]{4,3,2,1,0:T(8,128)} %bitcast.62), calls=%async_computation.2 | async-start | bytes 18874368 | tf_op jit(solution)/shard_map/all_to_all | solution.py:115
  92.9 15.5 %copy-start.1 = (f32[24,64,1536]{2,1,0:T(8,128)S(1)}, f32[24,64,1536]{2,1,0:T(8,128)}, u32[]{:S(2)}) copy-start(f32[24,64,1536]{2,1,0:T(8,128)} %add_select_fusion) | copy-start | bytes 28311556
  122.5 12.6 %collective-permute-start.4 = (f32[384,384]{1,0:T(8,128)}, f32[384,384]{1,0:T(8,128)S(1)}, u32[]{:S(2)}, u32[]{:S(2)}) collective-permute-start(f32[384,384]{1,0:T(8,128)} %get-tuple-element.20), channel_id=1, source_target_pairs={{0,24},{8,0},{16,8},{24,16},{1,25},{9,1},{17,9},{25,17},{2,26},{10... | collective-permute-start | bytes 1769480 | tf_op jit(solution)/shard_map/ppermute | solution.py:17
  123.9 24.5 %collective-permute-start.5 = (f32[384,384]{1,0:T(8,128)}, f32[384,384]{1,0:T(8,128)S(1)}, u32[]{:S(2)}, u32[]{:S(2)}) collective-permute-start(f32[384,384]{1,0:T(8,128)} %get-tuple-element.19), channel_id=1, source_target_pairs={{0,16},{8,24},{16,0},{24,8},{1,17},{9,25},{17,1},{25,9},{2,18},{10... | collective-permute-start | bytes 1769480 | tf_op jit(solution)/shard_map/ppermute | solution.py:17
  125.6 24.9 %collective-permute-start.6 = (f32[384,384]{1,0:T(8,128)S(1)}, f32[384,384]{1,0:T(8,128)S(1)}, u32[]{:S(2)}, u32[]{:S(2)}) collective-permute-start(f32[384,384]{1,0:T(8,128)S(1)} %get-tuple-element.18), channel_id=1, source_target_pairs={{0,8},{8,16},{16,24},{24,0},{1,9},{9,17},{17,25},{25,1},{2,10},{10... | collective-permute-start | bytes 1769480 | tf_op jit(solution)/shard_map/ppermute | solution.py:17
  150.8 1.7 copy-start.2
